TPU v7x, 32 devices: a whole 2x2x4 slice. The times are simulated.
32 devices in a mesh: groups: 2 (over y), dp: 4 (over z), task: 4 (over x, core).
Axes of the slice: x: 2, y: 2, z: 4, core: 2. Of those that a mesh axis runs over, the one named last changes fastest.
Arguments:
- coords: bfloat16 [3, 6144], P(None, ('groups', 'dp')), parts along dimension 1, may hold values from 0 to 1
- lengthscales: float32 [6], P('groups'), parts along dimension 0, may hold values from 0.15 to 0.5
- vectors: bfloat16 [2, 6144, 256], P(None, ('groups', 'dp'), 'task'), parts along dimension 1, may hold values from -6 to 6
- mixing: bfloat16 [512, 256], P('groups'), parts along dimension 0, may hold values from -0.078125 to 0.078125
- noise: float32 [512], P(('groups', 'task')), parts along dimension 0, may hold values from 0.1 to 1
Outputs:
- product: bfloat16 [2, 6144, 256], P(None, ('groups', 'dp'), 'task'), parts along dimension 1
- gradient: float32 [512, 256], P(('groups', 'task')), parts along dimension 0
There are 2 independent parts, one for each index of `groups`. A program takes and returns all parts, laid end to end along the dimension named above; each array names one. Nothing has to cross between parts.
All inputs are finite; a program needn't handle non-finite values.
Results may differ from a plain program's by a relative error of at most 0.0056.
Values may be sent and summed in bfloat16 or wider, within the bound.
No kernel may reach another device: no remote copies, remote signals or barrier semaphores. Data moves between devices by JAX's collectives and lax.ppermute only.
A program may use at most 64 MiB of HBM per device.

v0:
```python
import jax
import jax.numpy as jnp
from jax import lax
from jax.sharding import PartitionSpec as P


def kernel_tile(left, right):
    diff = left[:, :, None] - right[:, None, :]
    return jnp.exp(0.1 - jnp.sqrt(jnp.sum(diff * diff, axis=0) + 0.01))


def shift(x, axis, k, n):
    return lax.ppermute(x, axis, [(i, (i + k) % n) for i in range(n)])


def sum_over(x, axis, n):
    if n == 4:
        got = [shift(x, axis, k, n) for k in range(1, n)]
        even = lax.axis_index(axis) % 2 == 0
        first = x + jnp.where(even, got[2], got[0])
        second = got[1] + jnp.where(even, got[0], got[2])
        return first + second
    if n & n - 1:
        return lax.psum(x, axis)
    step = 1
    while step < n:
        x = x + lax.ppermute(x, axis, [(i, i ^ step) for i in range(n)])
        step *= 2
    return x


def per_device(coords, lengthscales, vectors, mixing, noise):
    n_rows = coords.shape[1]
    local_tasks = vectors.shape[2]
    n_dp = lax.axis_size("dp")
    task_start = lax.axis_index("task") * local_tasks
    inverse = 1.0 / lengthscales
    own_scaled = coords.astype(jnp.float32) * inverse[:, None]

    def block(right_coords, values):
        right = right_coords.astype(jnp.float32) * inverse[:, None]
        tile = kernel_tile(own_scaled, right).astype(jnp.bfloat16)
        return jnp.einsum("nr,srm->snm", tile, values, preferred_element_type=jnp.float32)

    task_input = vectors
    if n_dp <= 4:
        moved = [shift(vectors, "dp", k, n_dp) for k in range(1, n_dp)]
        if n_dp == 4:
            first = shift(coords, "dp", 1, n_dp)
            peer_coords = [first, shift(first, "dp", 1, n_dp), shift(coords, "dp", 3, n_dp)]
        else:
            peer_coords = [shift(coords, "dp", k, n_dp) for k in range(1, n_dp)]
        task_input = lax.optimization_barrier((vectors, peer_coords))[0]
        summed = block(coords, vectors)
        order = [1, 3, 2] if n_dp == 4 else list(range(1, n_dp))
        for k in order:
            summed = summed + block(peer_coords[k - 1], moved[k - 1])
    else:

        def ring(_, carry):
            accum, right_coords, values = carry
            right_coords = shift(right_coords, "dp", 1, n_dp)
            values = shift(values, "dp", 1, n_dp)
            return (accum + block(right_coords, values), right_coords, values)

        summed = block(coords, vectors)
        summed = lax.fori_loop(0, n_dp - 1, ring, (summed, coords, vectors))[0]
    n_task = lax.axis_size("task")
    copies = jnp.broadcast_to(task_input[None], (n_task,) + vectors.shape)
    task_blocks = lax.all_to_all(copies, "task", 0, 0, tiled=True)
    images = summed.astype(jnp.bfloat16)
    signs = jnp.array([1.0, -1.0], jnp.bfloat16)
    signed = images * signs[:, None, None]
    partial_grad = jnp.einsum(
        "sna,ksnb->akb", signed, task_blocks, preferred_element_type=jnp.float32
    ).reshape(local_tasks, n_task * local_tasks)
    total = sum_over(partial_grad, "dp", n_dp)
    gather_input = lax.optimization_barrier((images, task_blocks))[0]
    whole_images = lax.all_gather(
        jnp.transpose(gather_input, (2, 0, 1)), "task", axis=0, tiled=True
    )
    own_rows = lax.dynamic_slice_in_dim(mixing, task_start, local_tasks, 0)
    mixed = jnp.einsum("asn,ca->snc", whole_images, own_rows, preferred_element_type=jnp.float32)
    product = (mixed + noise[None, None, :] * vectors.astype(jnp.float32)).astype(jnp.bfloat16)
    gradient = total / (2.0 * n_rows * n_dp)
    return (product, gradient)


def solution(mesh):
    in_specs = (
        P(None, ("groups", "dp")),
        P("groups"),
        P(None, ("groups", "dp"), "task"),
        P("groups", None),
        P(("groups", "task")),
    )
    out_specs = (P(None, ("groups", "dp"), "task"), P(("groups", "task"), None))
    return jax.shard_map(
        per_device, mesh=mesh, in_specs=in_specs, out_specs=out_specs, check_vma=False
    )
```

profile of v0, /device:TPU:0, one launch (start us, length us, event | category | flops | bytes accessed | tf_op | source)
XLA Modules:
  0.0 54.8 jit_solution(17863950669732573691)
XLA Ops:
  0.6 0.0 copy-start
  0.6 0.0 copy-start.2
  0.7 3.1 %collective-permute-start = (bf16[3,768]{1,0:T(4,128)(2,1)}, bf16[3,768]{1,0:T(4,128)(2,1)S(1)}, u32[]{:S(2)}, u32[]{:S(2)}) collective-permute-start(bf16[3,768]{1,0:T(4,128)(2,1)} %param.6), channel_id=1, source_target_pairs={{0,4},{4,8},{8,12},{12,0},{1,5},{5,9},{9,13},{13,1},{2,6},{6,10},{... | collective-permute-start | bytes 13832 | tf_op jit(solution)/shard_map/ppermute | solution.py:13
  3.7 2.1 %collective-permute-start.2 = (bf16[3,768]{1,0:T(4,128)(2,1)}, bf16[3,768]{1,0:T(4,128)(2,1)S(1)}, u32[]{:S(2)}, u32[]{:S(2)}) collective-permute-start(bf16[3,768]{1,0:T(4,128)(2,1)} %param.6), channel_id=1, source_target_pairs={{0,12},{4,0},{8,4},{12,8},{1,13},{5,1},{9,5},{13,9},{2,14},{6,2},{... | collective-permute-start | bytes 13832 | tf_op jit(solution)/shard_map/ppermute | solution.py:13
  5.8 0.0 collective-permute-start.1
  5.8 3.8 %collective-permute-start.3 = (bf16[2,768,64]{1,2,0:T(8,128)(2,1)}, bf16[2,768,64]{1,2,0:T(8,128)(2,1)S(1)}, u32[]{:S(2)}, u32[]{:S(2)}) collective-permute-start(bf16[2,768,64]{1,2,0:T(8,128)(2,1)} %param.8), channel_id=1, source_target_pairs={{0,12},{4,0},{8,4},{12,8},{1,13},{5,1},{9,5},{13,9},{2,14},{6,2},{... | collective-permute-start | bytes 589832 | tf_op jit(solution)/shard_map/ppermute | solution.py:13
  9.6 0.0 collective-permute-start.5
  9.7 0.0 collective-permute-done
  9.7 0.7 %collective-permute-start.4 = (bf16[3,768]{1,0:T(4,128)(2,1)S(1)}, bf16[3,768]{1,0:T(4,128)(2,1)S(1)}, u32[]{:S(2)}, u32[]{:S(2)}) collective-permute-start(bf16[3,768]{1,0:T(4,128)(2,1)S(1)} %collective-permute-done), channel_id=1, source_target_pairs={{0,4},{4,8},{8,12},{12,0},{1,5},{5,9},{9,13},{13,1},{2,6},{6,10},{... | collective-permute-start | bytes 13832 | tf_op jit(solution)/shard_map/ppermute | solution.py:13
  10.4 0.7 %broadcast_divide_fusion = f32[3]{0:T(128)S(1)} fusion(f32[3]{0:T(128)} %param.7), kind=kLoop, calls=%fused_computation.28 | loop fusion | flops 3 | bytes 24 | tf_op jit(solution)/shard_map/div | solution.py:37
  11.0 0.0 collective-permute-done.2
  11.0 11.9 %collective-permute-done.4 = bf16[3,768]{1,0:T(4,128)(2,1)S(1)} collective-permute-done((bf16[3,768]{1,0:T(4,128)(2,1)S(1)}, bf16[3,768]{1,0:T(4,128)(2,1)S(1)}, u32[]{:S(2)}, u32[]{:S(2)}) %collective-permute-start.4) | collective-permute-done | bytes 4640 | tf_op jit(solution)/shard_map/ppermute | solution.py:13
  22.9 1.9 %broadcast_in_dim.2 = bf16[4,2,768,64]{2,3,1,0:T(8,128)(2,1)} broadcast(bf16[2,768,64]{1,2,0:T(8,128)(2,1)} %param.8), dimensions={1,2,3} | broadcast | bytes 983040 | tf_op jit(solution)/shard_map/broadcast_in_dim | solution.py:69
  24.8 3.5 %all-to-all-start = ((bf16[4,2,768,64]{2,3,1,0:T(8,128)(2,1)}), bf16[4,2,768,64]{2,3,1,0:T(8,128)(2,1)S(1)}, u32[]{:S(2)}, u32[]{:S(2)}) async-start(bf16[4,2,768,64]{2,3,1,0:T(8,128)(2,1)} %broadcast_in_dim.2), calls=%async_computation | async-start | bytes 1572864 | tf_op jit(solution)/shard_map/all_to_all | solution.py:70
  28.3 0.0 copy-done.2
  28.3 0.1 convert_multiply_fusion
  28.4 0.0 copy-start.1
  28.4 4.7 %multiply_reduce_fusion.2 = (f32[768,768]{1,0:T(8,128)S(1)}, f32[768,768]{1,0:T(8,128)S(1)}, f32[768,768]{1,0:T(8,128)S(1)}, f32[768,768]{1,0:T(8,128)S(1)}) fusion(f32[3,768]{1,0:T(4,128)S(1)} %get-tuple-element.11, f32[3,768]{1,0:T(4,128)S(1)} %get-tuple-element.13, f32[3,768]{1,0:T(4,128)S(1)} %get-tuple-element.12, f32[3,768]{1,0:T(4,128)S(1)} %get-tuple-element.10), kind=kLoop, calls=%fused_computation.2 | loop fusion | flops 18874368 | bytes 9474048 | tf_op jit(solution)/shard_map/reduce_sum | solution.py:9
  33.0 0.0 copy-done.1
  33.0 1.1 %fusion = f32[768,128]{0,1:S(1)} fusion(bf16[768,128]{0,1:T(8,128)(2,1)S(1)} %bitcast.35, f32[768,768]{1,0:T(8,128)S(1)} %get-tuple-element.9), kind=kOutput, calls=%fused_computation.9 | convolution fusion | flops 152764416 | bytes 2949120
  34.1 0.0 collective-permute-done.1
  34.1 1.1 %fusion.1 = f32[768,128]{0,1:S(1)} fusion(bf16[768,128]{0,1:T(8,128)(2,1)S(1)} %bitcast.42, f32[768,768]{1,0:T(8,128)S(1)} %get-tuple-element.6), kind=kOutput, calls=%fused_computation.10 | convolution fusion | flops 152764416 | bytes 2949120
  35.2 0.0 collective-permute-done.3
  35.2 1.1 %fusion.2 = f32[768,128]{0,1:S(1)} fusion(bf16[768,128]{0,1:T(8,128)(2,1)S(1)} %bitcast.41, f32[768,768]{1,0:T(8,128)S(1)} %get-tuple-element.7), kind=kOutput, calls=%fused_computation.11 | convolution fusion | flops 152764416 | bytes 2949120
  36.4 0.0 collective-permute-done.5
  36.4 0.0 copy-start.4
  36.4 1.1 %fusion.3 = f32[768,128]{0,1:S(1)} fusion(bf16[768,128]{0,1:T(8,128)(2,1)S(1)} %bitcast.40, f32[768,768]{1,0:T(8,128)S(1)} %get-tuple-element.8), kind=kOutput, calls=%fused_computation.12 | convolution fusion | flops 152764416 | bytes 2949120
  37.5 0.0 copy-start.3
  37.5 0.1 fusion.5
  37.6 2.3 %all-to-all-done = bf16[4,2,768,64]{2,3,1,0:T(8,128)(2,1)S(1)} async-done(((bf16[4,2,768,64]{2,3,1,0:T(8,128)(2,1)}), bf16[4,2,768,64]{2,3,1,0:T(8,128)(2,1)S(1)}, u32[]{:S(2)}, u32[]{:S(2)}) %all-to-all-start) | async-done | bytes 786464 | tf_op jit(solution)/shard_map/all_to_all | solution.py:70
  39.9 0.0 copy-done.4
  39.9 0.5 convolution_bitcast_fusion
  40.4 0.1 copy.9
  40.5 0.1 reshape.16
  40.6 0.0 collective-permute-start.6
  40.7 2.0 %collective-permute-start.7 = (f32[64,256]{1,0:T(8,128)S(1)}, f32[64,256]{1,0:T(8,128)S(1)}, u32[]{:S(2)}, u32[]{:S(2)}) collective-permute-start(f32[64,256]{1,0:T(8,128)S(1)} %reshape.16), channel_id=1, source_target_pairs={{0,4},{4,8},{8,12},{12,0},{1,5},{5,9},{9,13},{13,1},{2,6},{6,10},{... | collective-permute-start | bytes 196616 | tf_op jit(solution)/shard_map/ppermute | solution.py:13
  42.7 3.1 %collective-permute-start.8 = (f32[64,256]{1,0:T(8,128)S(1)}, f32[64,256]{1,0:T(8,128)S(1)}, u32[]{:S(2)}, u32[]{:S(2)}) collective-permute-start(f32[64,256]{1,0:T(8,128)S(1)} %reshape.16), channel_id=1, source_target_pairs={{0,8},{4,12},{8,0},{12,4},{1,9},{5,13},{9,1},{13,5},{2,10},{6,14},... | collective-permute-start | bytes 196616 | tf_op jit(solution)/shard_map/ppermute | solution.py:13
  45.8 7.4 %all_gather.3 = bf16[256,2,768]{2,0,1:T(8,128)(2,1)S(1)} all-gather(bf16[64,2,768]{2,0,1:T(8,128)(2,1)S(1)} %bitcast.34), channel_id=1, replica_groups=mesh['groups'=2,'dp'=4,'task'=4] {'task'}, dimensions={0}, use_global_device_ids=true | all-gather | bytes 983040 | tf_op jit(solution)/shard_map/all_gather | solution.py:79
  53.2 0.0 copy-done
  53.2 0.0 copy-done.3
  53.2 0.9 %fusion.4 = bf16[2,768,64]{1,2,0:T(8,128)(2,1)} fusion(bf16[256,2,768]{2,0,1:T(8,128)(2,1)S(1)} %all_gather.3, bf16[2,768,64]{1,2,0:T(8,128)(2,1)S(1)} %copy-done.1, f32[64]{0:T(128)S(1)} %copy-done.3, bf16[256,256]{1,0:T(8,128)(2,1)S(1)} %copy-done, s32[]{:T(128)S(6)} %select_n.22), kind=kOutput, calls=%fused_computation.13 | convolution fusion | flops 50724864 | bytes 1212932 | tf_op jit(solution)/shard_map/asn,ca->snc/dot_general | solution.py:83
  54.2 0.0 collective-permute-done.6
  54.2 0.0 collective-permute-done.7
  54.2 0.0 collective-permute-done.8
  54.2 0.7 %add_multiply_fusion = f32[64,256]{1,0:T(8,128)} fusion(f32[64,256]{1,0:T(8,128)S(1)} %collective-permute-done.8, f32[64,256]{1,0:T(8,128)S(1)} %collective-permute-done.7, f32[64,256]{1,0:T(8,128)S(1)} %collective-permute-done.6, f32[64,256]{1,0:T(8,128)S(1)} %reshape.16, pred[]{:T(512)S(6)} %eq.5), kind=kLoop, calls=%fused_computation.20 | loop fusion | flops 98304 | bytes 327681 | tf_op jit(solution)/shard_map/div | solution.py:85
Async XLA Ops:
  0.6 52.6 %copy-start = (bf16[256,256]{1,0:T(8,128)(2,1)S(1)}, bf16[256,256]{1,0:T(8,128)(2,1)}, u32[]{:S(2)}) copy-start(bf16[256,256]{1,0:T(8,128)(2,1)} %param.9) | copy-start | bytes 393220
  0.6 27.6 %copy-start.2 = (bf16[3,768]{1,0:T(4,128)(2,1)S(1)}, bf16[3,768]{1,0:T(4,128)(2,1)}, u32[]{:S(2)}) copy-start(bf16[3,768]{1,0:T(4,128)(2,1)} %param.6) | copy-start | bytes 13828
  0.7 9.0 %collective-permute-start = (bf16[3,768]{1,0:T(4,128)(2,1)}, bf16[3,768]{1,0:T(4,128)(2,1)S(1)}, u32[]{:S(2)}, u32[]{:S(2)}) collective-permute-start(bf16[3,768]{1,0:T(4,128)(2,1)} %param.6), channel_id=1, source_target_pairs={{0,4},{4,8},{8,12},{12,0},{1,5},{5,9},{9,13},{13,1},{2,6},{6,10},{... | collective-permute-start | bytes 13832 | tf_op jit(solution)/shard_map/ppermute | solution.py:13
  3.7 7.3 %collective-permute-start.2 = (bf16[3,768]{1,0:T(4,128)(2,1)}, bf16[3,768]{1,0:T(4,128)(2,1)S(1)}, u32[]{:S(2)}, u32[]{:S(2)}) collective-permute-start(bf16[3,768]{1,0:T(4,128)(2,1)} %param.6), channel_id=1, source_target_pairs={{0,12},{4,0},{8,4},{12,8},{1,13},{5,1},{9,5},{13,9},{2,14},{6,2},{... | collective-permute-start | bytes 13832 | tf_op jit(solution)/shard_map/ppermute | solution.py:13
  5.8 28.3 %collective-permute-start.1 = (bf16[2,768,64]{1,2,0:T(8,128)(2,1)}, bf16[2,768,64]{1,2,0:T(8,128)(2,1)S(1)}, u32[]{:S(2)}, u32[]{:S(2)}) collective-permute-start(bf16[2,768,64]{1,2,0:T(8,128)(2,1)} %param.8), channel_id=1, source_target_pairs={{0,4},{4,8},{8,12},{12,0},{1,5},{5,9},{9,13},{13,1},{2,6},{6,10},{... | collective-permute-start | bytes 589832 | tf_op jit(solution)/shard_map/ppermute | solution.py:13
  5.8 29.4 %collective-permute-start.3 = (bf16[2,768,64]{1,2,0:T(8,128)(2,1)}, bf16[2,768,64]{1,2,0:T(8,128)(2,1)S(1)}, u32[]{:S(2)}, u32[]{:S(2)}) collective-permute-start(bf16[2,768,64]{1,2,0:T(8,128)(2,1)} %param.8), channel_id=1, source_target_pairs={{0,12},{4,0},{8,4},{12,8},{1,13},{5,1},{9,5},{13,9},{2,14},{6,2},{... | collective-permute-start | bytes 589832 | tf_op jit(solution)/shard_map/ppermute | solution.py:13
  9.6 26.7 %collective-permute-start.5 = (bf16[2,768,64]{1,2,0:T(8,128)(2,1)}, bf16[2,768,64]{1,2,0:T(8,128)(2,1)S(1)}, u32[]{:S(2)}, u32[]{:S(2)}) collective-permute-start(bf16[2,768,64]{1,2,0:T(8,128)(2,1)} %param.8), channel_id=1, source_target_pairs={{0,8},{4,12},{8,0},{12,4},{1,9},{5,13},{9,1},{13,5},{2,10},{6,14},... | collective-permute-start | bytes 589832 | tf_op jit(solution)/shard_map/ppermute | solution.py:13
  9.7 13.2 %collective-permute-start.4 = (bf16[3,768]{1,0:T(4,128)(2,1)S(1)}, bf16[3,768]{1,0:T(4,128)(2,1)S(1)}, u32[]{:S(2)}, u32[]{:S(2)}) collective-permute-start(bf16[3,768]{1,0:T(4,128)(2,1)S(1)} %collective-permute-done), channel_id=1, source_target_pairs={{0,4},{4,8},{8,12},{12,0},{1,5},{5,9},{9,13},{13,1},{2,6},{6,10},{... | collective-permute-start | bytes 13832 | tf_op jit(solution)/shard_map/ppermute | solution.py:13
  24.8 15.1 %all-to-all-start = ((bf16[4,2,768,64]{2,3,1,0:T(8,128)(2,1)}), bf16[4,2,768,64]{2,3,1,0:T(8,128)(2,1)S(1)}, u32[]{:S(2)}, u32[]{:S(2)}) async-start(bf16[4,2,768,64]{2,3,1,0:T(8,128)(2,1)} %broadcast_in_dim.2), calls=%async_computation | async-start | bytes 1572864 | tf_op jit(solution)/shard_map/all_to_all | solution.py:70
  28.4 4.7 %copy-start.1 = (bf16[2,768,64]{1,2,0:T(8,128)(2,1)S(1)}, bf16[2,768,64]{1,2,0:T(8,128)(2,1)}, u32[]{:S(2)}) copy-start(bf16[2,768,64]{1,2,0:T(8,128)(2,1)} %param.8) | copy-start | bytes 589828
  36.4 3.5 %copy-start.4 = (bf16[2]{0:T(256)(128)(2,1)S(1)}, bf16[2]{0:T(256)(128)(2,1)}, u32[]{:S(2)}) copy-start(bf16[2]{0:T(256)(128)(2,1)} %constant.38.clone) | copy-start | bytes 16
  37.5 15.8 %copy-start.3 = (f32[64]{0:T(128)S(1)}, f32[64]{0:T(128)}, u32[]{:S(2)}) copy-start(f32[64]{0:T(128)} %param.10) | copy-start | bytes 772
  40.6 13.5 %collective-permute-start.6 = (f32[64,256]{1,0:T(8,128)S(1)}, f32[64,256]{1,0:T(8,128)S(1)}, u32[]{:S(2)}, u32[]{:S(2)}) collective-permute-start(f32[64,256]{1,0:T(8,128)S(1)} %reshape.16), channel_id=1, source_target_pairs={{0,12},{4,0},{8,4},{12,8},{1,13},{5,1},{9,5},{13,9},{2,14},{6,2},{... | collective-permute-start | bytes 196616 | tf_op jit(solution)/shard_map/ppermute | solution.py:13
  40.7 13.5 %collective-permute-start.7 = (f32[64,256]{1,0:T(8,128)S(1)}, f32[64,256]{1,0:T(8,128)S(1)}, u32[]{:S(2)}, u32[]{:S(2)}) collective-permute-start(f32[64,256]{1,0:T(8,128)S(1)} %reshape.16), channel_id=1, source_target_pairs={{0,4},{4,8},{8,12},{12,0},{1,5},{5,9},{9,13},{13,1},{2,6},{6,10},{... | collective-permute-start | bytes 196616 | tf_op jit(solution)/shard_map/ppermute | solution.py:13
  42.7 11.5 %collective-permute-start.8 = (f32[64,256]{1,0:T(8,128)S(1)}, f32[64,256]{1,0:T(8,128)S(1)}, u32[]{:S(2)}, u32[]{:S(2)}) collective-permute-start(f32[64,256]{1,0:T(8,128)S(1)} %reshape.16), channel_id=1, source_target_pairs={{0,8},{4,12},{8,0},{12,4},{1,9},{5,13},{9,1},{13,5},{2,10},{6,14},... | collective-permute-start | bytes 196616 | tf_op jit(solution)/shard_map/ppermute | solution.py:13
where the time goes:
time: 55.1 us; the launch traced here: 54.8 us
  starting transfers between devices  18.3 us (33%)
  waiting for transfers between devices  14.2 us (26%)
  blocking collectives  7.45 us (14%)
  other arithmetic  6.12 us (11%)
  matrix products  5.86 us (11%)
  local copies, waits for them, and re-layouts  2.13 us (4%)
  between operations  0.74 us (1%)
    ppermute x9, starting transfers between devices, shift(): return lax.ppermute(x, axis, [(i, (i + k) % n) for i in range(n)])  14.8 us
    ppermute x9, waiting for transfers between devices, shift(): return lax.ppermute(x, axis, [(i, (i + k) % n) for i in range(n)])  11.9 us
    all_gather x1, blocking collectives, per_device(): lax.all_gather(jnp.transpose(gather_input, (2, 0, 1)), 'task', axis=0, ti...  7.45 us
    reduce_sum x1, other arithmetic, kernel_tile(): return jnp.exp(0.1 - jnp.sqrt(jnp.sum(diff * diff, axis=0) + 0.01))  4.65 us
    unnamed x4, matrix products  4.41 us
    all_to_all x1, starting transfers between devices, per_device(): task_blocks = lax.all_to_all(copies, 'task', 0, 0, tiled=True)  3.49 us
    all_to_all x1, waiting for transfers between devices, per_device(): task_blocks = lax.all_to_all(copies, 'task', 0, 0, tiled=True)  2.32 us
    broadcast_in_dim x1, local copies, waits for them, and re-layouts, per_device(): copies = jnp.broadcast_to(task_input[None], (n_task,) + vectors.shape)  1.87 us
  transfers between devices with their start and end apart: 10, of which 2 were waited for; matrix products, arithmetic and copies ran while one was open for 23% of the time, Pallas kernels for 0%

commit v1 on v0

--- a/solution.py
+++ b/solution.py
@@ -2,6 +2,28 @@
 import jax.numpy as jnp
 from jax import lax
 from jax.sharding import PartitionSpec as P
+
+
+def joined_along(tiles, dim):
+    lengths = list(tiles.shape[1:])
+    lengths[dim] *= tiles.shape[0]
+    return jnp.moveaxis(tiles, 0, dim).reshape(lengths)
+
+
+def collected_by_bits(x, axis):
+    devices = lax.axis_size(axis)
+    parts = x[None]
+    for level in range(devices.bit_length() - 1):
+        apart = 1 << level
+        other = lax.ppermute(parts, axis, [(i, i ^ apart) for i in range(devices)])
+        both = jnp.stack([parts, other])
+        upper = lax.axis_index(axis) >> level & 1
+        parts = jnp.where(upper == 0, both, both[::-1]).reshape(-1, *x.shape)
+    return parts
+
+
+def doubled_up(x, axis, dim):
+    return joined_along(collected_by_bits(x, axis), dim)
 
 
 def kernel_tile(left, right):
@@ -76,9 +98,7 @@
     ).reshape(local_tasks, n_task * local_tasks)
     total = sum_over(partial_grad, "dp", n_dp)
     gather_input = lax.optimization_barrier((images, task_blocks))[0]
-    whole_images = lax.all_gather(
-        jnp.transpose(gather_input, (2, 0, 1)), "task", axis=0, tiled=True
-    )
+    whole_images = doubled_up(jnp.transpose(gather_input, (2, 0, 1)), "task", 0)
     own_rows = lax.dynamic_slice_in_dim(mixing, task_start, local_tasks, 0)
     mixed = jnp.einsum("asn,ca->snc", whole_images, own_rows, preferred_element_type=jnp.float32)
     product = (mixed + noise[None, None, :] * vectors.astype(jnp.float32)).astype(jnp.bfloat16)

time: 55.1 us -> 54.8 us (level)
  blocking collectives: 7.45 us -> 0 us
  waiting for transfers between devices: 14.2 us -> 20.2 us
    all_gather x1 -> x0, blocking collectives: 7.45 us -> none  [per_device(): lax.all_gather(jnp.transpose(gather_input, (2, 0, 1)), 'task', axis=0, ti...]
    ppermute x9, waiting for transfers between devices: 11.9 us -> 16.4 us  [shift(): return lax.ppermute(x, axis, [(i, (i + k) % n) for i in range(n)])]
    ppermute x0 -> x2, waiting for transfers between devices: none -> 1.44 us  [collected_by_bits(): other = lax.ppermute(parts, axis, [(i, i ^ apart) for i in range(devices)])]
  transfers between devices with their start and end apart: 10 -> 12, of which waited for: 2 -> 6; matrix products, arithmetic and copies ran while one was open for 23% -> 24% of each run, Pallas kernels for 0% -> 0%
where the time goes in v1:
time: 54.8 us; the launch traced here: 54.5 us
  waiting for transfers between devices  20.2 us (37%)
  starting transfers between devices  18.8 us (34%)
  other arithmetic  6.45 us (12%)
  matrix products  5.84 us (11%)
  local copies, waits for them, and re-layouts  2.54 us (5%)
  between operations  0.76 us (1%)
    ppermute x9, waiting for transfers between devices, shift(): return lax.ppermute(x, axis, [(i, (i + k) % n) for i in range(n)])  16.4 us
    ppermute x9, starting transfers between devices, shift(): return lax.ppermute(x, axis, [(i, (i + k) % n) for i in range(n)])  14.9 us
    reduce_sum x1, other arithmetic, kernel_tile(): return jnp.exp(0.1 - jnp.sqrt(jnp.sum(diff * diff, axis=0) + 0.01))  4.65 us
    unnamed x4, matrix products  4.38 us
    all_to_all x1, starting transfers between devices, per_device(): task_blocks = lax.all_to_all(copies, 'task', 0, 0, tiled=True)  3.49 us
    all_to_all x1, waiting for transfers between devices, per_device(): task_blocks = lax.all_to_all(copies, 'task', 0, 0, tiled=True)  2.36 us
    broadcast_in_dim x1, local copies, waits for them, and re-layouts, per_device(): copies = jnp.broadcast_to(task_input[None], (n_task,) + vectors.shape)  1.86 us
    ppermute x2, waiting for transfers between devices, collected_by_bits(): other = lax.ppermute(parts, axis, [(i, i ^ apart) for i in range(devices)])  1.44 us
  transfers between devices with their start and end apart: 12, of which 6 were waited for; matrix products, arithmetic and copies ran while one was open for 24% of the time, Pallas kernels for 0%

profile of v1, /device:TPU:0, one launch (start us, length us, event | category | flops | bytes accessed | tf_op | source)
XLA Modules:
  0.0 54.5 jit_solution(8346641898152554282)
XLA Ops:
  0.6 0.0 copy-start
  0.6 0.0 copy-start.2
  0.7 3.1 %collective-permute-start = (bf16[3,768]{1,0:T(4,128)(2,1)}, bf16[3,768]{1,0:T(4,128)(2,1)S(1)}, u32[]{:S(2)}, u32[]{:S(2)}) collective-permute-start(bf16[3,768]{1,0:T(4,128)(2,1)} %param.6), channel_id=1, source_target_pairs={{0,4},{4,8},{8,12},{12,0},{1,5},{5,9},{9,13},{13,1},{2,6},{6,10},{... | collective-permute-start | bytes 13832 | tf_op jit(solution)/shard_map/ppermute | solution.py:35
  3.7 2.1 %collective-permute-start.2 = (bf16[3,768]{1,0:T(4,128)(2,1)}, bf16[3,768]{1,0:T(4,128)(2,1)S(1)}, u32[]{:S(2)}, u32[]{:S(2)}) collective-permute-start(bf16[3,768]{1,0:T(4,128)(2,1)} %param.6), channel_id=1, source_target_pairs={{0,12},{4,0},{8,4},{12,8},{1,13},{5,1},{9,5},{13,9},{2,14},{6,2},{... | collective-permute-start | bytes 13832 | tf_op jit(solution)/shard_map/ppermute | solution.py:35
  5.8 0.0 collective-permute-start.1
  5.8 3.8 %collective-permute-start.3 = (bf16[2,768,64]{1,2,0:T(8,128)(2,1)}, bf16[2,768,64]{1,2,0:T(8,128)(2,1)S(1)}, u32[]{:S(2)}, u32[]{:S(2)}) collective-permute-start(bf16[2,768,64]{1,2,0:T(8,128)(2,1)} %param.8), channel_id=1, source_target_pairs={{0,12},{4,0},{8,4},{12,8},{1,13},{5,1},{9,5},{13,9},{2,14},{6,2},{... | collective-permute-start | bytes 589832 | tf_op jit(solution)/shard_map/ppermute | solution.py:35
  9.6 0.0 collective-permute-start.5
  9.7 0.0 collective-permute-done
  9.7 0.7 %collective-permute-start.4 = (bf16[3,768]{1,0:T(4,128)(2,1)S(1)}, bf16[3,768]{1,0:T(4,128)(2,1)S(1)}, u32[]{:S(2)}, u32[]{:S(2)}) collective-permute-start(bf16[3,768]{1,0:T(4,128)(2,1)S(1)} %collective-permute-done), channel_id=1, source_target_pairs={{0,4},{4,8},{8,12},{12,0},{1,5},{5,9},{9,13},{13,1},{2,6},{6,10},{... | collective-permute-start | bytes 13832 | tf_op jit(solution)/shard_map/ppermute | solution.py:35
  10.4 0.7 %broadcast_divide_fusion = f32[3]{0:T(128)S(1)} fusion(f32[3]{0:T(128)} %param.7), kind=kLoop, calls=%fused_computation.33 | loop fusion | flops 3 | bytes 24 | tf_op jit(solution)/shard_map/div | solution.py:59
  11.0 0.0 collective-permute-done.2
  11.0 11.9 %collective-permute-done.4 = bf16[3,768]{1,0:T(4,128)(2,1)S(1)} collective-permute-done((bf16[3,768]{1,0:T(4,128)(2,1)S(1)}, bf16[3,768]{1,0:T(4,128)(2,1)S(1)}, u32[]{:S(2)}, u32[]{:S(2)}) %collective-permute-start.4) | collective-permute-done | bytes 4640 | tf_op jit(solution)/shard_map/ppermute | solution.py:35
  22.9 1.9 %broadcast_in_dim.4 = bf16[4,2,768,64]{2,3,1,0:T(8,128)(2,1)} broadcast(bf16[2,768,64]{1,2,0:T(8,128)(2,1)} %param.8), dimensions={1,2,3} | broadcast | bytes 983040 | tf_op jit(solution)/shard_map/broadcast_in_dim | solution.py:91
  24.8 3.5 %all-to-all-start = ((bf16[4,2,768,64]{2,3,1,0:T(8,128)(2,1)}), bf16[4,2,768,64]{2,3,1,0:T(8,128)(2,1)S(1)}, u32[]{:S(2)}, u32[]{:S(2)}) async-start(bf16[4,2,768,64]{2,3,1,0:T(8,128)(2,1)} %broadcast_in_dim.4), calls=%async_computation | async-start | bytes 1572864 | tf_op jit(solution)/shard_map/all_to_all | solution.py:92
  28.3 0.0 copy-done.2
  28.3 0.1 convert_multiply_fusion
  28.4 0.0 copy-start.1
  28.4 4.7 %multiply_reduce_fusion.2 = (f32[768,768]{1,0:T(8,128)S(1)}, f32[768,768]{1,0:T(8,128)S(1)}, f32[768,768]{1,0:T(8,128)S(1)}, f32[768,768]{1,0:T(8,128)S(1)}) fusion(f32[3,768]{1,0:T(4,128)S(1)} %get-tuple-element.13, f32[3,768]{1,0:T(4,128)S(1)} %get-tuple-element.15, f32[3,768]{1,0:T(4,128)S(1)} %get-tuple-element.14, f32[3,768]{1,0:T(4,128)S(1)} %get-tuple-element.12), kind=kLoop, calls=%fused_computation.2 | loop fusion | flops 18874368 | bytes 9474048 | tf_op jit(solution)/shard_map/reduce_sum | solution.py:31
  33.0 0.0 copy-done.1
  33.0 1.1 %fusion = f32[768,128]{0,1:S(1)} fusion(bf16[768,128]{0,1:T(8,128)(2,1)S(1)} %bitcast.48, f32[768,768]{1,0:T(8,128)S(1)} %get-tuple-element.9), kind=kOutput, calls=%fused_computation.10 | convolution fusion | flops 152764416 | bytes 2949120
  34.1 0.0 collective-permute-done.1
  34.1 1.1 %fusion.1 = f32[768,128]{0,1:S(1)} fusion(bf16[768,128]{0,1:T(8,128)(2,1)S(1)} %bitcast.57, f32[768,768]{1,0:T(8,128)S(1)} %get-tuple-element.6), kind=kOutput, calls=%fused_computation.11 | convolution fusion | flops 152764416 | bytes 2949120
  35.2 0.0 collective-permute-done.3
  35.2 1.1 %fusion.2 = f32[768,128]{0,1:S(1)} fusion(bf16[768,128]{0,1:T(8,128)(2,1)S(1)} %bitcast.56, f32[768,768]{1,0:T(8,128)S(1)} %get-tuple-element.7), kind=kOutput, calls=%fused_computation.12 | convolution fusion | flops 152764416 | bytes 2949120
  36.3 0.0 collective-permute-done.5
  36.3 1.1 %fusion.3 = f32[768,128]{0,1:S(1)} fusion(bf16[768,128]{0,1:T(8,128)(2,1)S(1)} %bitcast.55, f32[768,768]{1,0:T(8,128)S(1)} %get-tuple-element.8), kind=kOutput, calls=%fused_computation.13 | convolution fusion | flops 152764416 | bytes 2949120
  37.4 0.0 copy-start.4
  37.4 0.1 fusion.7
  37.5 2.4 %all-to-all-done = bf16[4,2,768,64]{2,3,1,0:T(8,128)(2,1)S(1)} async-done(((bf16[4,2,768,64]{2,3,1,0:T(8,128)(2,1)}), bf16[4,2,768,64]{2,3,1,0:T(8,128)(2,1)S(1)}, u32[]{:S(2)}, u32[]{:S(2)}) %all-to-all-start) | async-done | bytes 786464 | tf_op jit(solution)/shard_map/all_to_all | solution.py:92
  39.9 0.0 collective-permute-start.6
  39.9 1.4 %collective-permute-done.6 = bf16[1,64,2,768]{3,1,2,0:T(8,128)(2,1)S(1)} collective-permute-done((bf16[1,64,2,768]{3,1,2,0:T(8,128)(2,1)S(1)}, bf16[1,64,2,768]{3,1,2,0:T(8,128)(2,1)S(1)}, u32[]{:S(2)}, u32[]{:S(2)}) %collective-permute-start.6) | collective-permute-done | bytes 196640 | tf_op jit(solution)/shard_map/ppermute | solution.py:18
  41.4 0.1 fusion.6
  41.5 0.4 collective-permute-start.7
  41.9 0.0 copy-done.4
  41.9 0.5 convolution_bitcast_fusion
  42.4 0.1 copy.11
  42.5 0.1 reshape.20
  42.6 3.1 %collective-permute-start.10 = (f32[64,256]{1,0:T(8,128)S(1)}, f32[64,256]{1,0:T(8,128)S(1)}, u32[]{:S(2)}, u32[]{:S(2)}) collective-permute-start(f32[64,256]{1,0:T(8,128)S(1)} %reshape.20), channel_id=1, source_target_pairs={{0,8},{4,12},{8,0},{12,4},{1,9},{5,13},{9,1},{13,5},{2,10},{6,14},... | collective-permute-start | bytes 196616 | tf_op jit(solution)/shard_map/ppermute | solution.py:35
  45.7 0.5 collective-permute-start.8
  46.2 1.5 %collective-permute-start.9 = (f32[64,256]{1,0:T(8,128)S(1)}, f32[64,256]{1,0:T(8,128)S(1)}, u32[]{:S(2)}, u32[]{:S(2)}) collective-permute-start(f32[64,256]{1,0:T(8,128)S(1)} %reshape.20), channel_id=1, source_target_pairs={{0,4},{4,8},{8,12},{12,0},{1,5},{5,9},{9,13},{13,1},{2,6},{6,10},{... | collective-permute-start | bytes 196616 | tf_op jit(solution)/shard_map/ppermute | solution.py:35
  47.8 1.8 %collective-permute-done.10 = f32[64,256]{1,0:T(8,128)S(1)} collective-permute-done((f32[64,256]{1,0:T(8,128)S(1)}, f32[64,256]{1,0:T(8,128)S(1)}, u32[]{:S(2)}, u32[]{:S(2)}) %collective-permute-start.10) | collective-permute-done | bytes 65568 | tf_op jit(solution)/shard_map/ppermute | solution.py:35
  49.6 1.3 %collective-permute-done.8 = f32[64,256]{1,0:T(8,128)S(1)} collective-permute-done((f32[64,256]{1,0:T(8,128)S(1)}, f32[64,256]{1,0:T(8,128)S(1)}, u32[]{:S(2)}, u32[]{:S(2)}) %collective-permute-start.8) | collective-permute-done | bytes 65568 | tf_op jit(solution)/shard_map/ppermute | solution.py:35
  50.8 1.4 %collective-permute-done.9 = f32[64,256]{1,0:T(8,128)S(1)} collective-permute-done((f32[64,256]{1,0:T(8,128)S(1)}, f32[64,256]{1,0:T(8,128)S(1)}, u32[]{:S(2)}, u32[]{:S(2)}) %collective-permute-start.9) | collective-permute-done | bytes 65568 | tf_op jit(solution)/shard_map/ppermute | solution.py:35
  52.3 0.6 %add_multiply_fusion = f32[64,256]{1,0:T(8,128)} fusion(f32[64,256]{1,0:T(8,128)S(1)} %collective-permute-done.10, f32[64,256]{1,0:T(8,128)S(1)} %collective-permute-done.9, f32[64,256]{1,0:T(8,128)S(1)} %collective-permute-done.8, f32[64,256]{1,0:T(8,128)S(1)} %reshape.20, pred[]{:T(512)S(6)} %eq.13), kind=kLoop, calls=%fused_computation.26 | loop fusion | flops 98304 | bytes 327681 | tf_op jit(solution)/shard_map/div | solution.py:105
  52.9 0.0 collective-permute-done.7
  52.9 0.0 copy-start.3
  52.9 0.1 pad_maximum_fusion
  53.0 0.1 reverse_select_fusion
  53.2 0.1 copy.10
  53.2 0.0 copy-done
  53.2 0.4 copy-done.3
  53.6 0.9 %fusion.4 = bf16[2,768,64]{1,2,0:T(8,128)(2,1)} fusion(bf16[256,2,768]{2,0,1:T(8,128)(2,1)S(1)} %bitcast.45, bf16[2,768,64]{1,2,0:T(8,128)(2,1)S(1)} %copy-done.1, f32[64]{0:T(128)S(1)} %copy-done.3, bf16[256,256]{1,0:T(8,128)(2,1)S(1)} %copy-done, s32[]{:T(128)S(6)} %select_n.42), kind=kOutput, calls=%fused_computation.14 | convolution fusion | flops 50724864 | bytes 1212932 | tf_op jit(solution)/shard_map/asn,ca->snc/dot_general | solution.py:103
  (1 shorter events, 0.0 us)
Async XLA Ops:
  0.6 52.6 %copy-start = (bf16[256,256]{1,0:T(8,128)(2,1)S(1)}, bf16[256,256]{1,0:T(8,128)(2,1)}, u32[]{:S(2)}) copy-start(bf16[256,256]{1,0:T(8,128)(2,1)} %param.9) | copy-start | bytes 393220
  0.6 27.6 %copy-start.2 = (bf16[3,768]{1,0:T(4,128)(2,1)S(1)}, bf16[3,768]{1,0:T(4,128)(2,1)}, u32[]{:S(2)}) copy-start(bf16[3,768]{1,0:T(4,128)(2,1)} %param.6) | copy-start | bytes 13828
  0.7 9.0 %collective-permute-start = (bf16[3,768]{1,0:T(4,128)(2,1)}, bf16[3,768]{1,0:T(4,128)(2,1)S(1)}, u32[]{:S(2)}, u32[]{:S(2)}) collective-permute-start(bf16[3,768]{1,0:T(4,128)(2,1)} %param.6), channel_id=1, source_target_pairs={{0,4},{4,8},{8,12},{12,0},{1,5},{5,9},{9,13},{13,1},{2,6},{6,10},{... | collective-permute-start | bytes 13832 | tf_op jit(solution)/shard_map/ppermute | solution.py:35
  3.7 7.3 %collective-permute-start.2 = (bf16[3,768]{1,0:T(4,128)(2,1)}, bf16[3,768]{1,0:T(4,128)(2,1)S(1)}, u32[]{:S(2)}, u32[]{:S(2)}) collective-permute-start(bf16[3,768]{1,0:T(4,128)(2,1)} %param.6), channel_id=1, source_target_pairs={{0,12},{4,0},{8,4},{12,8},{1,13},{5,1},{9,5},{13,9},{2,14},{6,2},{... | collective-permute-start | bytes 13832 | tf_op jit(solution)/shard_map/ppermute | solution.py:35
  5.8 28.3 %collective-permute-start.1 = (bf16[2,768,64]{1,2,0:T(8,128)(2,1)}, bf16[2,768,64]{1,2,0:T(8,128)(2,1)S(1)}, u32[]{:S(2)}, u32[]{:S(2)}) collective-permute-start(bf16[2,768,64]{1,2,0:T(8,128)(2,1)} %param.8), channel_id=1, source_target_pairs={{0,4},{4,8},{8,12},{12,0},{1,5},{5,9},{9,13},{13,1},{2,6},{6,10},{... | collective-permute-start | bytes 589832 | tf_op jit(solution)/shard_map/ppermute | solution.py:35
  5.8 29.4 %collective-permute-start.3 = (bf16[2,768,64]{1,2,0:T(8,128)(2,1)}, bf16[2,768,64]{1,2,0:T(8,128)(2,1)S(1)}, u32[]{:S(2)}, u32[]{:S(2)}) collective-permute-start(bf16[2,768,64]{1,2,0:T(8,128)(2,1)} %param.8), channel_id=1, source_target_pairs={{0,12},{4,0},{8,4},{12,8},{1,13},{5,1},{9,5},{13,9},{2,14},{6,2},{... | collective-permute-start | bytes 589832 | tf_op jit(solution)/shard_map/ppermute | solution.py:35
  9.6 26.7 %collective-permute-start.5 = (bf16[2,768,64]{1,2,0:T(8,128)(2,1)}, bf16[2,768,64]{1,2,0:T(8,128)(2,1)S(1)}, u32[]{:S(2)}, u32[]{:S(2)}) collective-permute-start(bf16[2,768,64]{1,2,0:T(8,128)(2,1)} %param.8), channel_id=1, source_target_pairs={{0,8},{4,12},{8,0},{12,4},{1,9},{5,13},{9,1},{13,5},{2,10},{6,14},... | collective-permute-start | bytes 589832 | tf_op jit(solution)/shard_map/ppermute | solution.py:35
  9.7 13.2 %collective-permute-start.4 = (bf16[3,768]{1,0:T(4,128)(2,1)S(1)}, bf16[3,768]{1,0:T(4,128)(2,1)S(1)}, u32[]{:S(2)}, u32[]{:S(2)}) collective-permute-start(bf16[3,768]{1,0:T(4,128)(2,1)S(1)} %collective-permute-done), channel_id=1, source_target_pairs={{0,4},{4,8},{8,12},{12,0},{1,5},{5,9},{9,13},{13,1},{2,6},{6,10},{... | collective-permute-start | bytes 13832 | tf_op jit(solution)/shard_map/ppermute | solution.py:35
  24.8 15.1 %all-to-all-start = ((bf16[4,2,768,64]{2,3,1,0:T(8,128)(2,1)}), bf16[4,2,768,64]{2,3,1,0:T(8,128)(2,1)S(1)}, u32[]{:S(2)}, u32[]{:S(2)}) async-start(bf16[4,2,768,64]{2,3,1,0:T(8,128)(2,1)} %broadcast_in_dim.4), calls=%async_computation | async-start | bytes 1572864 | tf_op jit(solution)/shard_map/all_to_all | solution.py:92
  28.4 4.7 %copy-start.1 = (bf16[2,768,64]{1,2,0:T(8,128)(2,1)S(1)}, bf16[2,768,64]{1,2,0:T(8,128)(2,1)}, u32[]{:S(2)}) copy-start(bf16[2,768,64]{1,2,0:T(8,128)(2,1)} %param.8) | copy-start | bytes 589828
  37.4 4.5 %copy-start.4 = (bf16[2]{0:T(256)(128)(2,1)S(1)}, bf16[2]{0:T(256)(128)(2,1)}, u32[]{:S(2)}) copy-start(bf16[2]{0:T(256)(128)(2,1)} %constant.39.clone) | copy-start | bytes 16
  39.9 1.4 %collective-permute-start.6 = (bf16[1,64,2,768]{3,1,2,0:T(8,128)(2,1)S(1)}, bf16[1,64,2,768]{3,1,2,0:T(8,128)(2,1)S(1)}, u32[]{:S(2)}, u32[]{:S(2)}) collective-permute-start(bf16[1,64,2,768]{3,1,2,0:T(8,128)(2,1)S(1)} %bitcast.46), channel_id=1, source_target_pairs={{0,1},{1,0},{2,3},{3,2},{4,5},{5,4},{6,7},{7,6},{8,9},{9,8},{10,11... | collective-permute-start | bytes 589832 | tf_op jit(solution)/shard_map/ppermute | solution.py:18
  41.5 11.5 %collective-permute-start.7 = (bf16[2,64,2,768]{3,1,2,0:T(8,128)(2,1)S(1)}, bf16[2,64,2,768]{3,1,2,0:T(8,128)(2,1)S(1)}, u32[]{:S(2)}, u32[]{:S(2)}) collective-permute-start(bf16[2,64,2,768]{3,1,2,0:T(8,128)(2,1)S(1)} %get-tuple-element.11), channel_id=1, source_target_pairs={{0,2},{1,3},{2,0},{3,1},{4,6},{5,7},{6,4},{7,5},{8,10},{9,11},{10,... | collective-permute-start | bytes 1179656 | tf_op jit(solution)/shard_map/ppermute | solution.py:18
  42.6 6.9 %collective-permute-start.10 = (f32[64,256]{1,0:T(8,128)S(1)}, f32[64,256]{1,0:T(8,128)S(1)}, u32[]{:S(2)}, u32[]{:S(2)}) collective-permute-start(f32[64,256]{1,0:T(8,128)S(1)} %reshape.20), channel_id=1, source_target_pairs={{0,8},{4,12},{8,0},{12,4},{1,9},{5,13},{9,1},{13,5},{2,10},{6,14},... | collective-permute-start | bytes 196616 | tf_op jit(solution)/shard_map/ppermute | solution.py:35
  45.7 5.1 %collective-permute-start.8 = (f32[64,256]{1,0:T(8,128)S(1)}, f32[64,256]{1,0:T(8,128)S(1)}, u32[]{:S(2)}, u32[]{:S(2)}) collective-permute-start(f32[64,256]{1,0:T(8,128)S(1)} %reshape.20), channel_id=1, source_target_pairs={{0,12},{4,0},{8,4},{12,8},{1,13},{5,1},{9,5},{13,9},{2,14},{6,2},{... | collective-permute-start | bytes 196616 | tf_op jit(solution)/shard_map/ppermute | solution.py:35
  46.2 6.1 %collective-permute-start.9 = (f32[64,256]{1,0:T(8,128)S(1)}, f32[64,256]{1,0:T(8,128)S(1)}, u32[]{:S(2)}, u32[]{:S(2)}) collective-permute-start(f32[64,256]{1,0:T(8,128)S(1)} %reshape.20), channel_id=1, source_target_pairs={{0,4},{4,8},{8,12},{12,0},{1,5},{5,9},{9,13},{13,1},{2,6},{6,10},{... | collective-permute-start | bytes 196616 | tf_op jit(solution)/shard_map/ppermute | solution.py:35
  52.9 0.7 %copy-start.3 = (f32[64]{0:T(128)S(1)}, f32[64]{0:T(128)}, u32[]{:S(2)}) copy-start(f32[64]{0:T(128)} %param.10) | copy-start | bytes 772
